TPU v7x, 512 devices: a whole 4x8x8 slice. The times are simulated.
512 devices in a mesh: req: 64 (over x, z, core), tp: 8 (over y).
Axes of the slice: x: 4, y: 8, z: 8, core: 2. Of those that a mesh axis runs over, the one named last changes fastest.
Arguments:
- queries: bfloat16 [1280, 2048], P('req', 'tp')
- new_keys: bfloat16 [1280, 2048], P('req', 'tp'), may hold values from -6 to 6
- new_values: bfloat16 [1280, 2048], P('req', 'tp'), may hold values from -6 to 6
- cache_keys: bfloat16 [256, 384, 2048], P('req', None, 'tp'), may hold values from -6 to 6
- cache_values: bfloat16 [256, 384, 2048], P('req', None, 'tp'), may hold values from -6 to 6
- cache_lengths: int32 [256], P('req'), may hold values from 1 to 384, as said below
- hidden_in: bfloat16 [1280, 2048], P('req'), may hold values from -6 to 6
- out_weight: bfloat16 [2048, 2048], P('tp'), may hold values from -0.125 to 0.125
- norm_gain: float32 [2048], replicated, may hold values from 0.25 to 1.75
- routes: int32 [1280, 6], P('req'), may hold values from 0 to 63, all different within a row; in each aligned block of 20 rows (0 to 19, 20 to 39, ...) at most 3 rows name the same one
- route_gates: float32 [1280, 6], P('req'), may hold values from 0.05 to 0.5
- gate_weight: bfloat16 [64, 2048, 1408], P('req', None, 'tp'), may hold values from -0.125 to 0.125
- up_weight: bfloat16 [64, 2048, 1408], P('req', None, 'tp'), may hold values from -0.125 to 0.125
- down_weight: bfloat16 [64, 1408, 2048], P('req', 'tp'), may hold values from -0.15625 to 0.15625
Outputs:
- hidden_out: bfloat16 [1280, 2048], P('req', 'tp')
Inputs may be any that keep to these rules, and one draw needn't show every extreme that they name: `cache_lengths`: at least one request has all 384 slots live. `routes`: each token names 6 different experts; within each aligned block of 20 tokens (the tokens of one index of req) no expert is named more than 3 times.
All inputs are finite; a program needn't handle non-finite values.
Results may differ from a plain program's by a relative error of at most 0.008.
Values may be sent and summed in bfloat16 or wider, within the bound.
No kernel may reach another device: no remote copies, remote signals or barrier semaphores. Data moves between devices by JAX's collectives and lax.ppermute only.
A program may use at most 64 MiB of HBM per device.

v0:
```python
import jax
import jax.numpy as jnp
from jax import lax
from jax.sharding import PartitionSpec as P

HD = 128
EXPERTS = 64
POS = 5
CACHE = 384
CAP = 3


def slot_tables(local_routes, local_gates):
    flat_routes = local_routes.reshape(-1)
    expert_ids = jnp.arange(EXPERTS, dtype=jnp.int32)
    onehot = (flat_routes[:, None] == expert_ids[None, :]).astype(jnp.int32)
    before = jnp.cumsum(onehot, axis=0) - onehot
    ranks = jnp.sum(before * onehot, axis=1)
    slot_ids = (flat_routes * CAP + ranks).reshape(local_routes.shape)
    slot_range = jnp.arange(EXPERTS * CAP, dtype=jnp.int32)
    matches = slot_ids[None, :, :] == slot_range[:, None, None]
    dispatch = jnp.any(matches, axis=-1).astype(jnp.bfloat16)
    combine = jnp.sum(jnp.where(matches, local_gates[None, :, :], 0.0), axis=-1).T
    return (dispatch, combine)


def attend_local(queries, new_keys, new_values, cache_keys, cache_values, cache_lengths):
    req_count = cache_keys.shape[0]
    head_count = queries.shape[1] // HD
    all_keys = jnp.concatenate([cache_keys, new_keys.reshape(req_count, POS, -1)], axis=1).reshape(
        req_count, CACHE + POS, head_count, HD
    )
    all_values = jnp.concatenate(
        [cache_values, new_values.reshape(req_count, POS, -1)], axis=1
    ).reshape(req_count, CACHE + POS, head_count, HD)
    local_q = queries.reshape(req_count, POS, head_count, HD)
    scores = jnp.einsum(
        "rphd,rjhd->rhpj", local_q, all_keys, preferred_element_type=jnp.float32
    ) * HD ** (-0.5)
    key_pos = jnp.arange(CACHE + POS, dtype=jnp.int32)
    query_pos = jnp.arange(POS, dtype=jnp.int32)
    cache_live = key_pos[None, None, :] < cache_lengths[:, None, None]
    fresh_live = key_pos[None, None, :] - CACHE <= query_pos[None, :, None]
    live = jnp.where(key_pos[None, None, :] < CACHE, cache_live, fresh_live)
    scores = jnp.where(live[:, None, :, :], scores, -1e30)
    top = jnp.max(scores, axis=-1, keepdims=True)
    expo = jnp.exp(scores - top)
    weights = (expo / jnp.sum(expo, axis=-1, keepdims=True)).astype(jnp.bfloat16)
    attended = jnp.einsum(
        "rhpj,rjhd->rphd", weights, all_values, preferred_element_type=jnp.float32
    )
    return attended.astype(jnp.bfloat16).reshape(req_count * POS, head_count * HD)


def expert_apply(slot_rows, gate_weight, up_weight, down_weight):
    gated = jnp.einsum("secd,edf->secf", slot_rows, gate_weight, preferred_element_type=jnp.float32)
    upward = jnp.einsum("secd,edf->secf", slot_rows, up_weight, preferred_element_type=jnp.float32)
    activation = (jax.nn.silu(gated) * upward).astype(jnp.bfloat16)
    return jnp.einsum("secf,efd->secd", activation, down_weight, preferred_element_type=jnp.float32)


def local(
    queries,
    new_keys,
    new_values,
    cache_keys,
    cache_values,
    cache_lengths,
    hidden_in,
    out_weight,
    norm_gain,
    routes,
    route_gates,
    gate_weight,
    up_weight,
    down_weight,
):
    attended = attend_local(queries, new_keys, new_values, cache_keys, cache_values, cache_lengths)
    partial_value = jnp.dot(attended, out_weight, preferred_element_type=jnp.float32)
    model_width = partial_value.shape[1]
    tp_count = lax.axis_size("tp")
    columns = model_width // tp_count
    offset = lax.axis_index("tp") * columns
    holders = lax.axis_size("req")
    dispatch, combine = slot_tables(routes, route_gates)
    summed = lax.psum(partial_value, "tp") + hidden_in.astype(jnp.float32)
    mean_square = jnp.mean(summed * summed, axis=-1, keepdims=True)
    normed = (summed * lax.rsqrt(mean_square + 1e-06) * norm_gain[None, :]).astype(jnp.bfloat16)
    outbound = jnp.dot(dispatch, normed, preferred_element_type=jnp.float32).astype(jnp.bfloat16)
    outbound = outbound.reshape(holders, -1, CAP, model_width)
    produced = expert_apply(
        lax.all_to_all(outbound, "req", split_axis=0, concat_axis=0, tiled=True),
        gate_weight,
        up_weight,
        down_weight,
    )
    returned = lax.all_to_all(
        produced.astype(jnp.bfloat16), "req", split_axis=0, concat_axis=0, tiled=True
    ).astype(produced.dtype)
    expert_sum = jnp.dot(
        combine,
        returned.reshape(-1, model_width),
        precision=lax.Precision.HIGHEST,
        preferred_element_type=jnp.float32,
    )
    expert_cols = lax.psum_scatter(
        expert_sum.astype(jnp.bfloat16), "tp", scatter_dimension=1, tiled=True
    ).astype(jnp.float32)
    summed_cols = lax.dynamic_slice_in_dim(summed, offset, columns, 1)
    return (summed_cols + expert_cols).astype(jnp.bfloat16)


def solution(mesh):
    in_specs = (
        P("req", "tp"),
        P("req", "tp"),
        P("req", "tp"),
        P("req", None, "tp"),
        P("req", None, "tp"),
        P("req"),
        P("req", None),
        P("tp", None),
        P(),
        P("req", None),
        P("req", None),
        P("req", None, "tp"),
        P("req", None, "tp"),
        P("req", "tp", None),
    )
    out_specs = P("req", "tp")
    return jax.shard_map(local, mesh=mesh, in_specs=in_specs, out_specs=out_specs, check_vma=False)
```

profile of v0, /device:TPU:2, one launch (start us, length us, event | category | flops | bytes accessed | tf_op | source)
XLA Modules:
  0.0 220.3 jit_solution(8481350041058466535)
XLA Ops:
  6.5 0.0 all-reduce.2.cloned.1.call-start
  6.5 1.6 copy.64
  8.1 0.0 copy-start.4
  8.1 0.0 copy-start.9
  8.2 0.0 copy-start.5
  8.2 0.0 copy-start.1
  8.2 0.4 copy.65
  8.6 0.2 copy-done.4
  8.9 0.0 copy-done.9
  8.9 0.1 iota_compare_fusion.3
  9.0 0.3 copy-done.1
  9.3 0.4 copy.61
  9.7 0.0 copy-start.6
  9.7 0.4 copy.62
  10.1 0.3 copy-done.6
  10.4 0.6 fusion.71
  11.0 0.6 fusion.9
  11.7 0.0 copy-start.7
  11.7 0.9 fusion.76
  12.6 0.0 all-reduce.2.cloned.1.call-update
  12.7 0.0 copy-done.3
  12.7 0.1 copy.69
  12.8 0.1 eq.28
  12.9 0.1 fusion.38
  13.0 0.2 reduce_window_sum.11
  13.1 0.2 select_reduce_fusion.1
  13.3 0.1 reduce_sum.40
  13.4 0.1 copy.70
  13.5 0.1 fusion.33
  13.6 81.7 %all-reduce.2.cloned.1.call-done = f32[20,2048]{1,0:T(8,128)} async-done(((f32[20,2048]{1,0:T(8,128)}), f32[20,2048]{1,0:T(8,128)}) %all-reduce.2.cloned.1.call-update) | async-done | bytes 163856 | tf_op jit(solution)/shard_map/psum | solution.py:86
  95.3 0.0 copy-done.2
  95.3 1.1 multiply_reduce_fusion
  96.4 0.4 convolution_convert_fusion.1
  96.8 0.5 reshape.120
  97.4 0.0 copy-start.10
  97.4 37.8 %all_to_all.10 = bf16[64,1,3,2048]{3,2,1,0:T(4,128)(2,1)S(1)} all-to-all(bf16[64,1,3,2048]{3,2,1,0:T(4,128)(2,1)S(1)} %bitcast.79), channel_id=1, replica_groups=mesh['req'=64,'tp'=8] {'req'}, dimensions={0} | all-to-all | bytes 1572864 | tf_op jit(solution)/shard_map/all_to_all | solution.py:92
  135.2 1.0 convolution_bitcast_fusion.1
  136.2 2.6 %fusion.1 = bf16[64,1,3,2048]{3,0,2,1:T(8,128)(2,1)S(1)} fusion(bf16[1,176,2048]{2,1,0:T(8,128)(2,1)} %param.27, bf16[1,2048,176]{1,2,0:T(8,128)(2,1)} %param.26, bf16[64,1,3,2048]{3,2,1,0:T(4,128)(2,1)S(1)} %all_to_all.10, f32[64,1,3,176]{3,0,2,1:T(8,128)S(1)} %convolution_bitcast_fusion.1), kind=kOutput, calls=%fused_computation.3 | convolution fusion | flops 277420032 | bytes 3149824 | tf_op jit(solution)/shard_map/secf,efd->secd/dot_general | solution.py:59
  138.8 1.7 copy.73
  140.5 7.9 %all-to-all-start.1 = ((bf16[64,1,3,2048]{3,2,1,0:T(4,128)(2,1)}), bf16[64,1,3,2048]{3,2,1,0:T(4,128)(2,1)S(1)}, u32[]{:S(2)}, u32[]{:S(2)}) async-start(bf16[64,1,3,2048]{3,2,1,0:T(4,128)(2,1)} %copy.73), calls=%async_computation.1 | async-start | bytes 2097152 | tf_op jit(solution)/shard_map/all_to_all | solution.py:97
  148.4 0.0 reduce-scatter.2.cloned.1.call-start
  148.4 0.1 select_reduce_fusion
  148.5 26.8 %all-to-all-done.1 = bf16[64,1,3,2048]{3,2,1,0:T(4,128)(2,1)S(1)} async-done(((bf16[64,1,3,2048]{3,2,1,0:T(4,128)(2,1)}), bf16[64,1,3,2048]{3,2,1,0:T(4,128)(2,1)S(1)}, u32[]{:S(2)}, u32[]{:S(2)}) %all-to-all-start.1) | async-done | bytes 786464 | tf_op jit(solution)/shard_map/all_to_all | solution.py:97
  175.3 0.7 reshape.126
  176.0 1.1 convolution_convert_fusion.2
  177.1 0.0 reduce-scatter.2.cloned.1.call-update
  177.1 35.1 %reduce-scatter.2.cloned.1.call-done = bf16[20,256]{1,0:T(8,128)(2,1)} async-done(((bf16[20,2048]{1,0:T(8,128)(2,1)}), bf16[20,256]{1,0:T(8,128)(2,1)}) %reduce-scatter.2.cloned.1.call-update) | async-done | bytes 10256 | tf_op jit(solution)/shard_map/reduce_scatter | solution.py:106
  212.2 1.3 add_convert_fusion
  (23 shorter events, 0.2 us)
Async XLA Ops:
  6.5 5.2 %copy-start = (bf16[256,2048]{1,0:T(8,128)(2,1)S(1)}, bf16[256,2048]{1,0:T(8,128)(2,1)}, u32[]{:S(2)}) copy-start(bf16[256,2048]{1,0:T(8,128)(2,1)} %param.21) | copy-start | bytes 3145732
  6.5 88.8 %all-reduce.2.cloned.1.call-start = ((), (), s32[]{:S(2)}) async-start(), calls=%async_computation.3 | async-start | bytes 393216 | tf_op jit(solution)/shard_map/psum | solution.py:86
  8.1 0.7 copy-start.4
  8.1 0.7 copy-start.9
  8.2 0.8 copy-start.5
  8.2 1.1 copy-start.1
  9.7 0.7 copy-start.6
  11.6 1.1 copy-start.3
  11.6 83.7 %copy-start.2 = (bf16[20,2048]{1,0:T(8,128)(2,1)S(1)}, bf16[20,2048]{1,0:T(8,128)(2,1)}, u32[]{:S(2)}) copy-start(bf16[20,2048]{1,0:T(8,128)(2,1)} %param.20) | copy-start | bytes 245764
  11.7 84.7 %copy-start.7 = (f32[2048]{0:T(1024)S(1)}, f32[2048]{0:T(1024)}, u32[]{:S(2)}) copy-start(f32[2048]{0:T(1024)} %param.22) | copy-start | bytes 24580
  97.4 37.8 %copy-start.10 = (bf16[1,2048,176]{1,2,0:T(8,128)(2,1)S(1)}, bf16[1,2048,176]{1,2,0:T(8,128)(2,1)}, u32[]{:S(2)}) copy-start(bf16[1,2048,176]{1,2,0:T(8,128)(2,1)} %param.25) | copy-start | bytes 2162692
  140.5 8.0 %copy-start.8 = (f32[20,6]{0,1:T(8,128)S(1)}, f32[20,6]{0,1:T(8,128)}, u32[]{:S(2)}) copy-start(f32[20,6]{0,1:T(8,128)} %param.24) | copy-start | bytes 1444
  140.5 34.9 %all-to-all-start.1 = ((bf16[64,1,3,2048]{3,2,1,0:T(4,128)(2,1)}), bf16[64,1,3,2048]{3,2,1,0:T(4,128)(2,1)S(1)}, u32[]{:S(2)}, u32[]{:S(2)}) async-start(bf16[64,1,3,2048]{3,2,1,0:T(4,128)(2,1)} %copy.73), calls=%async_computation.1 | async-start | bytes 2097152 | tf_op jit(solution)/shard_map/all_to_all | solution.py:97
  148.4 63.8 %reduce-scatter.2.cloned.1.call-start = ((), (), s32[]{:S(2)}) async-start(), calls=%async_computation.4 | async-start | bytes 110592 | tf_op jit(solution)/shard_map/reduce_scatter | solution.py:106
Sparse Core Ops, SparseCore 0:
  12.8 82.4 all-reduce.1
  177.2 34.9 reduce-scatter.1
where the time goes:
time: 221 us; the launch traced here: 220 us
  waiting for transfers between devices  144 us (65%)
  blocking collectives  37.8 us (17%)
  between operations  13.7 us (6%)
  starting transfers between devices  7.95 us (4%)
  matrix products  7.21 us (3%)
  local copies, waits for them, and re-layouts  6.98 us (3%)
  other arithmetic  3.12 us (1%)
    psum x1, waiting for transfers between devices, local(): summed = lax.psum(partial_value, 'tp') + hidden_in.astype(jnp.float32)  81.7 us
    all_to_all x1, blocking collectives, local(): lax.all_to_all(outbound, 'req', split_axis=0, concat_axis=0, tiled=True)  37.8 us
    reduce_scatter x1, waiting for transfers between devices, local(): lax.psum_scatter(expert_sum.astype(jnp.bfloat16), 'tp', scatter_dimension...  35.1 us
    all_to_all x1, waiting for transfers between devices, local(): lax.all_to_all(produced.astype(jnp.bfloat16), 'req', split_axis=0, concat...  26.8 us
    all_to_all x1, starting transfers between devices, local(): lax.all_to_all(produced.astype(jnp.bfloat16), 'req', split_axis=0, concat...  7.9 us
  transfers between devices with their start and end apart: 3, of which 3 were waited for; matrix products, arithmetic and copies ran while one was open for 0% of the time, Pallas kernels for 0%

commit v1 on v0

--- a/solution.py
+++ b/solution.py
@@ -83,7 +83,8 @@
     offset = lax.axis_index("tp") * columns
     holders = lax.axis_size("req")
     dispatch, combine = slot_tables(routes, route_gates)
-    summed = lax.psum(partial_value, "tp") + hidden_in.astype(jnp.float32)
+    define_halves_for = lambda x0: jnp.sum(lax.all_gather(x0, axis_name="tp"), axis=0)
+    summed = define_halves_for(partial_value) + hidden_in.astype(jnp.float32)
     mean_square = jnp.mean(summed * summed, axis=-1, keepdims=True)
     normed = (summed * lax.rsqrt(mean_square + 1e-06) * norm_gain[None, :]).astype(jnp.bfloat16)
     outbound = jnp.dot(dispatch, normed, preferred_element_type=jnp.float32).astype(jnp.bfloat16)

time: 221 us -> 185 us (0.84)
  waiting for transfers between devices: 144 us -> 108 us
    psum x1 -> x0, waiting for transfers between devices: 81.7 us -> none  [local(): summed = lax.psum(partial_value, 'tp') + hidden_in.astype(jnp.float32)]
    all_gather x0 -> x1, waiting for transfers between devices: none -> 45.9 us  [local(): lax.all_gather(x0, axis_name='tp')]
  transfers between devices with their start and end apart: 3 -> 3, of which waited for: 3 -> 3; matrix products, arithmetic and copies ran while one was open for 0% -> 1% of each run, Pallas kernels for 0% -> 0%
where the time goes in v1:
time: 185 us; the launch traced here: 184 us
  waiting for transfers between devices  108 us (58%)
  blocking collectives  37.8 us (20%)
  between operations  13.7 us (7%)
  starting transfers between devices  7.82 us (4%)
  matrix products  7.2 us (4%)
  local copies, waits for them, and re-layouts  6.22 us (3%)
  other arithmetic  3.72 us (2%)
    all_gather x1, waiting for transfers between devices, local(): lax.all_gather(x0, axis_name='tp')  45.9 us
    all_to_all x1, blocking collectives, local(): lax.all_to_all(outbound, 'req', split_axis=0, concat_axis=0, tiled=True)  37.8 us
    reduce_scatter x1, waiting for transfers between devices, local(): lax.psum_scatter(expert_sum.astype(jnp.bfloat16), 'tp', scatter_dimension...  35.2 us
    all_to_all x1, waiting for transfers between devices, local(): lax.all_to_all(produced.astype(jnp.bfloat16), 'req', split_axis=0, concat...  26.8 us
    all_to_all x1, starting transfers between devices, local(): lax.all_to_all(produced.astype(jnp.bfloat16), 'req', split_axis=0, concat...  7.77 us
  transfers between devices with their start and end apart: 3, of which 3 were waited for; matrix products, arithmetic and copies ran while one was open for 1% of the time, Pallas kernels for 0%

profile of v1, /device:TPU:2, one launch (start us, length us, event | category | flops | bytes accessed | tf_op | source)
XLA Modules:
  0.0 184.3 jit_solution(8068088640754788358)
XLA Ops:
  6.5 0.0 all-gather.4.cloned.1.call-start
  6.5 0.0 copy-start.4
  6.6 0.0 copy-start.9
  6.6 0.0 copy-start.5
  6.6 0.0 copy-start.1
  6.6 1.6 copy.64
  8.2 0.4 copy.65
  8.7 0.1 iota_compare_fusion.3
  8.8 0.0 copy-start.6
  8.8 0.4 copy.61
  9.2 0.5 copy.62
  9.6 0.0 copy-done.6
  9.7 0.6 fusion.71
  10.3 0.6 fusion.9
  10.9 0.0 copy-done
  11.0 0.0 copy-start.2
  11.0 0.9 convolution_bitcast_fusion
  11.9 0.0 all-gather.4.cloned.1.call-update
  11.9 0.1 copy.69
  12.0 0.1 eq.28
  12.1 0.1 fusion.38
  12.2 0.2 reduce_window_sum.11
  12.4 0.2 select_reduce_fusion.1
  12.6 0.1 reduce_sum.50
  12.7 0.1 copy.70
  12.8 0.1 fusion.33
  12.9 45.9 %all-gather.4.cloned.1.call-done = f32[8,20,2048]{2,1,0:T(8,128)} async-done(((f32[1,20,2048]{2,1,0:T(8,128)}), f32[8,20,2048]{2,1,0:T(8,128)}) %all-gather.4.cloned.1.call-update) | async-done | bytes 1310736 | tf_op jit(solution)/shard_map/all_gather | solution.py:86
  58.7 1.5 reduce_sum.48
  60.2 0.1 multiply_reduce_fusion
  60.4 0.4 convolution_convert_fusion.1
  60.8 0.5 reshape.120
  61.4 0.0 copy-start.10
  61.4 37.8 %all_to_all.10 = bf16[64,1,3,2048]{3,2,1,0:T(4,128)(2,1)S(1)} all-to-all(bf16[64,1,3,2048]{3,2,1,0:T(4,128)(2,1)S(1)} %bitcast.81), channel_id=1, replica_groups=mesh['req'=64,'tp'=8] {'req'}, dimensions={0} | all-to-all | bytes 1572864 | tf_op jit(solution)/shard_map/all_to_all | solution.py:93
  99.2 0.0 copy-done.10
  99.2 1.0 convolution_bitcast_fusion.2
  100.2 2.6 %fusion.1 = bf16[64,1,3,2048]{3,0,2,1:T(8,128)(2,1)S(1)} fusion(bf16[1,176,2048]{2,1,0:T(8,128)(2,1)} %param.27, bf16[1,2048,176]{1,2,0:T(8,128)(2,1)} %param.26, bf16[64,1,3,2048]{3,2,1,0:T(4,128)(2,1)S(1)} %all_to_all.10, f32[64,1,3,176]{3,0,2,1:T(8,128)S(1)} %convolution_bitcast_fusion.2), kind=kOutput, calls=%fused_computation.3 | convolution fusion | flops 277420032 | bytes 3149824 | tf_op jit(solution)/shard_map/secf,efd->secd/dot_general | solution.py:59
  102.8 0.0 copy-start.8
  102.8 1.7 copy.73
  104.5 7.8 %all-to-all-start.1 = ((bf16[64,1,3,2048]{3,2,1,0:T(4,128)(2,1)}), bf16[64,1,3,2048]{3,2,1,0:T(4,128)(2,1)S(1)}, u32[]{:S(2)}, u32[]{:S(2)}) async-start(bf16[64,1,3,2048]{3,2,1,0:T(4,128)(2,1)} %copy.73), calls=%async_computation.1 | async-start | bytes 2097152 | tf_op jit(solution)/shard_map/all_to_all | solution.py:98
  112.2 0.0 reduce-scatter.2.cloned.1.call-start
  112.3 0.0 copy-done.8
  112.3 0.1 select_reduce_fusion
  112.4 26.8 %all-to-all-done.1 = bf16[64,1,3,2048]{3,2,1,0:T(4,128)(2,1)S(1)} async-done(((bf16[64,1,3,2048]{3,2,1,0:T(4,128)(2,1)}), bf16[64,1,3,2048]{3,2,1,0:T(4,128)(2,1)S(1)}, u32[]{:S(2)}, u32[]{:S(2)}) %all-to-all-start.1) | async-done | bytes 786464 | tf_op jit(solution)/shard_map/all_to_all | solution.py:98
  139.2 0.7 reshape.126
  139.9 1.1 convolution_convert_fusion.2
  140.9 0.0 reduce-scatter.2.cloned.1.call-update
  141.0 35.2 %reduce-scatter.2.cloned.1.call-done = bf16[20,256]{1,0:T(8,128)(2,1)} async-done(((bf16[20,2048]{1,0:T(8,128)(2,1)}), bf16[20,256]{1,0:T(8,128)(2,1)}) %reduce-scatter.2.cloned.1.call-update) | async-done | bytes 10256 | tf_op jit(solution)/shard_map/reduce_scatter | solution.py:107
  176.2 1.3 add_convert_fusion
  (24 shorter events, 0.2 us)
Async XLA Ops:
  6.5 4.4 %copy-start = (bf16[256,2048]{1,0:T(8,128)(2,1)S(1)}, bf16[256,2048]{1,0:T(8,128)(2,1)}, u32[]{:S(2)}) copy-start(bf16[256,2048]{1,0:T(8,128)(2,1)} %param.21) | copy-start | bytes 3145732
  6.5 52.2 %all-gather.4.cloned.1.call-start = ((), (), s32[]{:S(2)}) async-start(), calls=%async_computation.4 | async-start | bytes 1769472 | tf_op jit(solution)/shard_map/all_gather | solution.py:86
  6.5 2.1 %copy-start.4 = (bf16[20,256]{1,0:T(8,128)(2,1)S(1)}, bf16[20,256]{1,0:T(8,128)(2,1)}, u32[]{:S(2)}) copy-start(bf16[20,256]{1,0:T(8,128)(2,1)} %param.15) | copy-start | bytes 30724
  6.6 2.1 %copy-start.9 = (s32[4]{0:T(128)S(1)}, s32[4]{0:T(128)}, u32[]{:S(2)}) copy-start(s32[4]{0:T(128)} %param.19) | copy-start | bytes 52
  6.6 2.2 %copy-start.5 = (bf16[20,256]{1,0:T(8,128)(2,1)S(1)}, bf16[20,256]{1,0:T(8,128)(2,1)}, u32[]{:S(2)}) copy-start(bf16[20,256]{1,0:T(8,128)(2,1)} %param.14) | copy-start | bytes 30724
  6.6 2.2 %copy-start.1 = (bf16[4,384,256]{2,1,0:T(8,128)(2,1)S(1)}, bf16[4,384,256]{2,1,0:T(8,128)(2,1)}, u32[]{:S(2)}) copy-start(bf16[4,384,256]{2,1,0:T(8,128)(2,1)} %param.18) | copy-start | bytes 2359300
  8.8 0.8 copy-start.6
  10.3 1.7 copy-start.3
  11.0 49.3 %copy-start.2 = (bf16[20,2048]{1,0:T(8,128)(2,1)S(1)}, bf16[20,2048]{1,0:T(8,128)(2,1)}, u32[]{:S(2)}) copy-start(bf16[20,2048]{1,0:T(8,128)(2,1)} %param.20) | copy-start | bytes 245764
  11.9 48.5 %copy-start.7 = (f32[2048]{0:T(1024)S(1)}, f32[2048]{0:T(1024)}, u32[]{:S(2)}) copy-start(f32[2048]{0:T(1024)} %param.22) | copy-start | bytes 24580
  61.4 37.8 %copy-start.10 = (bf16[1,2048,176]{1,2,0:T(8,128)(2,1)S(1)}, bf16[1,2048,176]{1,2,0:T(8,128)(2,1)}, u32[]{:S(2)}) copy-start(bf16[1,2048,176]{1,2,0:T(8,128)(2,1)} %param.25) | copy-start | bytes 2162692
  102.8 9.5 %copy-start.8 = (f32[20,6]{0,1:T(8,128)S(1)}, f32[20,6]{0,1:T(8,128)}, u32[]{:S(2)}) copy-start(f32[20,6]{0,1:T(8,128)} %param.24) | copy-start | bytes 1444
  104.5 34.7 %all-to-all-start.1 = ((bf16[64,1,3,2048]{3,2,1,0:T(4,128)(2,1)}), bf16[64,1,3,2048]{3,2,1,0:T(4,128)(2,1)S(1)}, u32[]{:S(2)}, u32[]{:S(2)}) async-start(bf16[64,1,3,2048]{3,2,1,0:T(4,128)(2,1)} %copy.73), calls=%async_computation.1 | async-start | bytes 2097152 | tf_op jit(solution)/shard_map/all_to_all | solution.py:98
  112.2 63.9 %reduce-scatter.2.cloned.1.call-start = ((), (), s32[]{:S(2)}) async-start(), calls=%async_computation.3 | async-start | bytes 110592 | tf_op jit(solution)/shard_map/reduce_scatter | solution.py:107
Sparse Core Ops, SparseCore 0:
  12.0 46.6 all-gather.3
  141.1 35.0 reduce-scatter.1
